TPU v7x, 256 devices: a whole 4x4x8 slice. The times are simulated.
256 devices in a mesh: kv: 8 (over x, core), seq: 32 (over z, y).
Axes of the slice: x: 4, y: 4, z: 8, core: 2. Of those that a mesh axis runs over, the one named last changes fastest.
Arguments:
- hidden_states: bfloat16 [6144, 2048], P('seq')
- attn_gain: float32 [2048], replicated, may hold values from 0.5 to 1.5
- w_q: bfloat16 [2048, 2048], P(None, 'kv')
- w_k: bfloat16 [2048, 512], P(None, 'kv')
- w_v: bfloat16 [2048, 512], P(None, 'kv'), may hold values from -0.125 to 0.125
- w_o: bfloat16 [2048, 2048], P('kv'), may hold values from -0.125 to 0.125
- final_gain: float32 [2048], replicated, may hold values from 0.5 to 1.5
- w_head: bfloat16 [2048, 49408], P(None, ('kv', 'seq'))
- doc_lengths: int32 [26], replicated, may hold values from 1 to 3072, as said below
- target_ids: int32 [6144], replicated, may hold values from 0 to 49154, as said below
- vocab_mask: int32 [49408], P(('kv', 'seq')), may hold values from 0 to 1, as said below
Outputs:
- log_probs: float32 [6144], P('seq')
- entropies: float32 [6144], P('seq')
Inputs may be any that keep to these rules, and one draw needn't show every extreme that they name: `doc_lengths`: they sum to 6144; one is 3072, one more is over 1536, every other is under 64. `target_ids`: each names an entry whose vocab_mask is 1. `vocab_mask`: entries from 49155 on are 0.
All inputs are finite; a program needn't handle non-finite values.
Results may differ from a plain program's by a relative error of at most 0.0045.
Values may be sent and summed in bfloat16 or wider, within the bound.
No kernel may reach another device: no remote copies, remote signals or barrier semaphores. Data moves between devices by JAX's collectives and lax.ppermute only.
A program may use at most 128 MiB of HBM per device.

v0:
```python
import math
import jax
import jax.numpy as jnp
from jax import lax
from jax.sharding import PartitionSpec as P

HEAD_DIM = 64
ROPE_THETA = 10000000.0
NORM_EPS = 1e-05
NEG_FILL = -1e30
ATTN_SCALE = 0.015625
RESID_SCALE = 5.0
LOGIT_SCALE = 0.125


def rms_norm(values, gain_vec):
    return (
        values * lax.rsqrt(jnp.mean(values * values, axis=-1, keepdims=True) + NORM_EPS) * gain_vec
    )


def rotate(values, positions):
    half_dim = values.shape[-1] // 2
    inverse = jnp.exp(
        jnp.arange(half_dim, dtype=jnp.float32) * (-2.0 * math.log(ROPE_THETA) / values.shape[-1])
    )
    angles = positions.astype(jnp.float32)[:, None] * inverse[None, :]
    cos_val = jnp.cos(angles)[:, None, :]
    sine_val = jnp.sin(angles)[:, None, :]
    lower_half = values[..., :half_dim]
    upper_half = values[..., half_dim:]
    return jnp.concatenate(
        [
            lower_half * cos_val - upper_half * sine_val,
            upper_half * cos_val + lower_half * sine_val,
        ],
        axis=-1,
    )


def local(
    hidden_states,
    attn_gain,
    w_q,
    w_k,
    w_v,
    w_o,
    final_gain,
    w_head,
    doc_lengths,
    target_ids,
    vocab_mask,
):
    tok_rows = hidden_states.shape[0]
    seq_index = lax.axis_index("seq")
    kv_local = w_k.shape[1] // HEAD_DIM
    q_local = w_q.shape[1] // HEAD_DIM
    group_size = q_local // kv_local
    key_width = kv_local * HEAD_DIM
    stream = hidden_states.astype(jnp.float32)
    normed_in = rms_norm(stream, attn_gain).astype(jnp.bfloat16)
    queries = jnp.dot(normed_in, w_q, preferred_element_type=jnp.float32)
    key_proj = jnp.dot(normed_in, w_k, preferred_element_type=jnp.float32)
    value_proj = jnp.dot(normed_in, w_v, preferred_element_type=jnp.float32)
    token_pos = seq_index * tok_rows + jnp.arange(tok_rows, dtype=jnp.int32)
    doc_ends = jnp.cumsum(doc_lengths)
    doc_starts = doc_ends - doc_lengths
    doc_start = jnp.max(
        jnp.where(doc_starts[None, :] <= token_pos[:, None], doc_starts[None, :], 0), axis=1
    )
    positions = token_pos - doc_start
    rotated_q = rotate(queries.reshape(tok_rows, q_local, HEAD_DIM), positions).astype(jnp.bfloat16)
    rotated_q = rotated_q.reshape(tok_rows, kv_local, group_size, HEAD_DIM)
    rotated_k = rotate(key_proj.reshape(tok_rows, kv_local, HEAD_DIM), positions).astype(
        jnp.bfloat16
    )
    packed = jnp.concatenate(
        [rotated_k.reshape(tok_rows, key_width), value_proj.astype(jnp.bfloat16)], axis=1
    )
    earliest = doc_start[0]
    latest = token_pos[tok_rows - 1]
    initial = (
        jnp.full((kv_local, group_size, tok_rows), NEG_FILL, jnp.float32),
        jnp.zeros((kv_local, group_size, tok_rows), jnp.float32),
        jnp.zeros((kv_local, group_size, tok_rows, HEAD_DIM), jnp.float32),
    )
    shard_rows = lax.all_gather(packed, "seq", axis=0, tiled=True)
    offset = jnp.int32(0)
    row_count = shard_rows.shape[0]
    key_pos = jnp.arange(row_count, dtype=jnp.int32)

    def update(current):
        top_score, totals, context_sum = current
        key_rows = shard_rows[:, :key_width].reshape(row_count, kv_local, HEAD_DIM)
        value_rows = shard_rows[:, key_width:].reshape(row_count, kv_local, HEAD_DIM)
        scores = (
            jnp.einsum("tkgd,skd->kgts", rotated_q, key_rows, preferred_element_type=jnp.float32)
            * ATTN_SCALE
        )
        allowed = (key_pos[None, :] >= doc_start[:, None]) & (
            key_pos[None, :] <= token_pos[:, None]
        )
        scores = jnp.where(allowed, scores, NEG_FILL)
        new_top = jnp.maximum(top_score, jnp.max(scores, axis=-1))
        weights = jnp.where(allowed, jnp.exp(scores - new_top[..., None]), 0.0)
        rescale = jnp.exp(top_score - new_top)
        totals = jnp.sum(weights, axis=-1)
        context_sum = jnp.einsum(
            "kgts,skd->kgtd",
            weights.astype(jnp.bfloat16),
            value_rows,
            preferred_element_type=jnp.float32,
        )
        return (new_top, totals, context_sum)

    skip_piece = (offset + row_count <= earliest) | (offset > latest)
    top_score, totals, context_sum = lax.cond(skip_piece, lambda current: current, update, initial)
    context = (
        (context_sum / totals[..., None])
        .transpose(2, 0, 1, 3)
        .reshape(tok_rows, q_local * HEAD_DIM)
        .astype(jnp.bfloat16)
    )
    vocab_local = w_head.shape[1]
    flat_rank = lax.axis_index(("kv", "seq"))
    live_mask = vocab_mask == 1
    columns = flat_rank * vocab_local + jnp.arange(vocab_local, dtype=jnp.int32)
    attn_out = lax.psum(jnp.dot(context, w_o, preferred_element_type=jnp.float32), "kv")
    final_in = rms_norm(stream + RESID_SCALE * attn_out, final_gain).astype(jnp.bfloat16)
    head_shard_rows = lax.all_gather(final_in, "seq", axis=0, tiled=True)
    logits = jnp.dot(head_shard_rows, w_head, preferred_element_type=jnp.float32) * LOGIT_SCALE
    masked = jnp.where(live_mask[None, :], logits, NEG_FILL)
    top_row = jnp.max(masked, axis=1)
    shifted = jnp.where(live_mask[None, :], masked - top_row[:, None], 0.0)
    expw = jnp.where(live_mask[None, :], jnp.exp(shifted), 0.0)
    target = jnp.sum(jnp.where(target_ids[:, None] == columns[None, :], logits, 0.0), axis=1)
    row_stats = jnp.stack([top_row, jnp.sum(expw, axis=1), jnp.sum(expw * shifted, axis=1), target])
    top_all = lax.pmax(row_stats[0], ("kv", "seq"))
    rescale = jnp.exp(row_stats[0] - top_all)
    total_all, spread_all, target_all = lax.psum(
        (
            row_stats[1] * rescale,
            rescale * (row_stats[2] + (row_stats[0] - top_all) * row_stats[1]),
            row_stats[3],
        ),
        ("kv", "seq"),
    )
    log_prob = target_all - top_all - jnp.log(total_all)
    entropy = jnp.log(total_all) - spread_all / total_all
    log_probs = lax.dynamic_slice_in_dim(log_prob, seq_index * tok_rows, tok_rows, 0)
    entropies = lax.dynamic_slice_in_dim(entropy, seq_index * tok_rows, tok_rows, 0)
    return (log_probs, entropies)


def solution(mesh):
    in_specs = (
        P("seq", None),
        P(),
        P(None, "kv"),
        P(None, "kv"),
        P(None, "kv"),
        P("kv", None),
        P(),
        P(None, ("kv", "seq")),
        P(),
        P(),
        P(("kv", "seq")),
    )
    out_specs = (P("seq"), P("seq"))
    return jax.shard_map(local, mesh=mesh, in_specs=in_specs, out_specs=out_specs, check_vma=False)
```

profile of v0, /device:TPU:1, one launch (start us, length us, event | category | flops | bytes accessed | tf_op | source)
XLA Modules:
  0.0 718.2 jit_solution(9096987467154612652)
XLA Ops:
  7.3 1.5 fusion.16
  8.8 0.8 copy.22
  9.7 0.7 sub.45
  10.5 1.6 convolution_convert_fusion
  12.2 1.6 convolution_bitcast_fusion
  14.0 0.7 copy.23
  18.2 73.0 %all-gather.3.cloned.1.call-done = bf16[6144,128]{1,0:T(8,128)(2,1)} async-done(((bf16[192,128]{1,0:T(8,128)(2,1)}), bf16[6144,128]{1,0:T(8,128)(2,1)}) %all-gather.3.cloned.1.call-update) | async-done | bytes 1572880 | tf_op jit(solution)/shard_map/all_gather | solution.py:87
  91.2 21.4 %conditional.1 = (f32[1,4,192]{2,1,0:T(4,128)S(1)}, f32[1,4,192,64]{2,3,1,0:T(8,128)S(1)}) conditional(s32[]{:T(128)} %bitcast.9, (s32[6144]{0:T(1024)S(1)}, s32[6144]{0:T(1024)S(1)}, s32[192]{0:T(256)S(1)}, s32[192]{0:T(256)S(1)}, bf16[6144,128]{1,0:T(8,128)(2,1)}, /*index=5*/bf16[192,1,4,64]{0,3,2,1:T(8,128)(2,1)S(1)}) %tuple.16, () %tuple.17), branch_computations={%region_3.6_spmd, %region_6.7_spmd} | conditional | flops 1272839424 | bytes 66424336 | solution.py:117
  91.2 1.0 compare_and_fusion
  92.2 2.6 copy.25
  94.8 5.0 fusion
  99.8 6.3 fusion.7
  106.1 6.5 fusion.2
  112.6 1.6 fusion.37
  114.5 69.0 %all-reduce.4.cloned.1.call-done = f32[192,2048]{1,0:T(8,128)} async-done(((f32[192,2048]{1,0:T(8,128)}), f32[192,2048]{1,0:T(8,128)}) %all-reduce.4.cloned.1.call-update) | async-done | bytes 1572880 | tf_op jit(solution)/shard_map/psum | solution.py:128
  183.5 1.7 multiply_reduce_fusion.1
  185.2 2.6 multiply_convert_fusion
  188.0 184.3 %all-gather.5.cloned.1.call-done = bf16[6144,2048]{1,0:T(8,128)(2,1)} async-done(((bf16[192,2048]{1,0:T(8,128)(2,1)}), bf16[6144,2048]{1,0:T(8,128)(2,1)}) %all-gather.5.cloned.1.call-update) | async-done | bytes 25165840 | tf_op jit(solution)/shard_map/all_gather | solution.py:130
  372.3 14.4 %select_reduce_fusion.1 = (f32[6144]{0:T(1024)S(1)}, f32[6144,193]{0,1:T(8,128)}) fusion(pred[193]{0:T(512)(128)(4,1)S(1)} %broadcast_compare_fusion, bf16[6144,2048]{1,0:T(8,128)(2,1)} %all-gather.5.cloned.1.call-done, bf16[2048,193]{0,1:T(8,128)(2,1)S(1)} %copy-done.5), kind=kOutput, calls=%fused_computation.24 | convolution fusion | flops 4860555264 | bytes 30724288 | tf_op jit(solution)/shard_map/dot_general | solution.py:131
  386.7 75.4 %pmax.7 = f32[6144]{0:T(1024)S(1)} all-reduce(f32[6144]{0:T(1024)S(1)} %get-tuple-element.53), channel_id=1, replica_groups=mesh['kv'=8,'seq'=32] {'kv','seq'}, use_global_device_ids=true, to_apply=%region_12.13 | all-reduce | flops 6144 | bytes 49152 | tf_op jit(solution)/shard_map/pmax | solution.py:138
  462.1 4.9 multiply_reduce_fusion
  467.6 242.0 %all-reduce.6.cloned.1.call-done = (f32[6144]{0:T(1024)}, f32[6144]{0:T(1024)}, f32[6144]{0:T(1024)}) async-done(((f32[6144]{0:T(1024)}, f32[6144]{0:T(1024)}, f32[6144]{0:T(1024)}), (f32[6144]{0:T(1024)}, f32[6144]{0:T(1024)}, f32[6144]{0:T(1024)})) %all-reduce.6.cloned.1.call-update) | async-done | bytes 73744 | tf_op jit(solution)/shard_map/psum | solution.py:140
  709.6 0.7 log.4
  710.3 1.4 fusion.32
  (46 shorter events, 3.6 us)
Async XLA Ops:
  7.2 105.5 %copy-start = (bf16[256,2048]{1,0:T(8,128)(2,1)S(1)}, bf16[256,2048]{1,0:T(8,128)(2,1)}, u32[]{:S(2)}) copy-start(bf16[256,2048]{1,0:T(8,128)(2,1)} %param.18) | copy-start | bytes 3145732
  7.2 10.2 %copy-start.1 = (bf16[192,2048]{1,0:T(8,128)(2,1)S(1)}, bf16[192,2048]{1,0:T(8,128)(2,1)}, u32[]{:S(2)}) copy-start(bf16[192,2048]{1,0:T(8,128)(2,1)} %param.13) | copy-start | bytes 2359300
  7.2 10.2 %copy-start.6 = (f32[2048]{0:T(1024)S(1)}, f32[2048]{0:T(1024)}, u32[]{:S(2)}) copy-start(f32[2048]{0:T(1024)} %param.14) | copy-start | bytes 24580
  7.2 10.2 %copy-start.4 = (bf16[2048,256]{1,0:T(8,128)(2,1)S(1)}, bf16[2048,256]{1,0:T(8,128)(2,1)}, u32[]{:S(2)}) copy-start(bf16[2048,256]{1,0:T(8,128)(2,1)} %param.15) | copy-start | bytes 3145732
  7.2 84.0 %all-gather.3.cloned.1.call-start = ((), (), s32[]{:S(2)}) async-start(), calls=%async_computation | async-start | bytes 1622016 | tf_op jit(solution)/shard_map/all_gather | solution.py:87
  14.8 168.7 %all-reduce.4.cloned.1.call-start = ((), (), s32[]{:S(2)}) async-start(), calls=%async_computation.1 | async-start | bytes 3145728 | tf_op jit(solution)/shard_map/psum | solution.py:128
  112.6 72.7 %copy-start.3 = (f32[2048]{0:T(1024)S(1)}, f32[2048]{0:T(1024)}, u32[]{:S(2)}) copy-start(f32[2048]{0:T(1024)} %param.19) | copy-start | bytes 24580
  112.6 75.4 %copy-start.7 = (s32[193]{0:T(256)S(1)}, s32[193]{0:T(256)}, u32[]{:S(2)}) copy-start(s32[193]{0:T(256)} %param.23) | copy-start | bytes 2320
  112.6 259.7 %copy-start.5 = (bf16[2048,193]{0,1:T(8,128)(2,1)S(1)}, bf16[2048,193]{0,1:T(8,128)(2,1)}, u32[]{:S(2)}) copy-start(bf16[2048,193]{0,1:T(8,128)(2,1)} %param.20) | copy-start | bytes 2371588
  114.2 258.1 %all-gather.5.cloned.1.call-start = ((), (), s32[]{:S(2)}) async-start(), calls=%async_computation.2 | async-start | bytes 25952256 | tf_op jit(solution)/shard_map/all_gather | solution.py:130
  187.9 521.7 %all-reduce.6.cloned.1.call-start = ((), (), s32[]{:S(2)}) async-start(), calls=%async_computation.3 | async-start | bytes 147456 | tf_op jit(solution)/shard_map/psum | solution.py:140
  188.0 274.1 %copy-start.2 = (s32[6144]{0:T(1024)S(1)}, s32[6144]{0:T(1024)}, u32[]{:S(2)}) copy-start(s32[6144]{0:T(1024)} %param.22) | copy-start | bytes 73732
Sparse Core Ops, SparseCore 0:
  14.9 76.2 all-gather.2
  114.3 69.0 all-reduce.3
  188.0 184.2 all-gather.4
  467.7 241.7 all-reduce.5
where the time goes:
time: 719 us; the launch traced here: 718 us
  waiting for transfers between devices  568 us (79%)
  blocking collectives  75.4 us (10%)
  matrix products  31.1 us (4%)
  other arithmetic  21.7 us (3%)
  between operations  15.3 us (2%)
    psum x1, waiting for transfers between devices, local(): lax.psum((row_stats[1] * rescale, rescale * (row_stats[2] + (row_stats[0]...  242 us
    all_gather x1, waiting for transfers between devices, local(): head_shard_rows = lax.all_gather(final_in, 'seq', axis=0, tiled=True)  184 us
    pmax x1, blocking collectives, local(): top_all = lax.pmax(row_stats[0], ('kv', 'seq'))  75.4 us
    all_gather x1, waiting for transfers between devices, local(): shard_rows = lax.all_gather(packed, 'seq', axis=0, tiled=True)  73 us
    psum x1, waiting for transfers between devices, local(): lax.psum(jnp.dot(context, w_o, preferred_element_type=jnp.float32), 'kv')  69 us
    dot_general x1, matrix products, local(): jnp.dot(head_shard_rows, w_head, preferred_element_type=jnp.float32)  14.4 us
  transfers between devices with their start and end apart: 4, of which 4 were waited for; matrix products, arithmetic and copies ran while one was open for 0% of the time, Pallas kernels for 0%

commit v1 on v0

--- a/solution.py
+++ b/solution.py
@@ -3,6 +3,7 @@
 import jax.numpy as jnp
 from jax import lax
 from jax.sharding import PartitionSpec as P
+from jax.lax import all_to_all, axis_size
 
 HEAD_DIM = 64
 ROPE_THETA = 10000000.0
@@ -127,7 +128,9 @@
     columns = flat_rank * vocab_local + jnp.arange(vocab_local, dtype=jnp.int32)
     attn_out = lax.psum(jnp.dot(context, w_o, preferred_element_type=jnp.float32), "kv")
     final_in = rms_norm(stream + RESID_SCALE * attn_out, final_gain).astype(jnp.bfloat16)
-    head_shard_rows = lax.all_gather(final_in, "seq", axis=0, tiled=True)
+    head_shard_rows = jnp.concatenate(
+        all_to_all(jnp.stack([final_in] * axis_size("seq")), "seq", 0, 0), axis=0
+    )
     logits = jnp.dot(head_shard_rows, w_head, preferred_element_type=jnp.float32) * LOGIT_SCALE
     masked = jnp.where(live_mask[None, :], logits, NEG_FILL)
     top_row = jnp.max(masked, axis=1)

time: 719 us -> 1170 us (1.63)
  waiting for transfers between devices: 568 us -> 974 us
  blocking collectives: 75.4 us -> 101 us
    all_to_all x0 -> x1, waiting for transfers between devices: none -> 589 us  [local(): all_to_all(jnp.stack([final_in] * axis_size('seq')), 'seq', 0, 0)]
    all_gather x1 -> x0, waiting for transfers between devices: 184 us -> none  [local(): head_shard_rows = lax.all_gather(final_in, 'seq', axis=0, tiled=True)]
    pmax x1, blocking collectives: 75.4 us -> 101 us  [local(): top_all = lax.pmax(row_stats[0], ('kv', 'seq'))]
where the time goes in v1:
time: 1170 us
  waiting for transfers between devices  974 us (83%)
  blocking collectives  101 us (9%)
  matrix products  31.2 us (3%)
  other arithmetic  20.6 us (2%)
  between operations  15.3 us (1%)
  local copies, waits for them, and re-layouts  14.7 us (1%)
    all_to_all x1, waiting for transfers between devices, local(): all_to_all(jnp.stack([final_in] * axis_size('seq')), 'seq', 0, 0)  589 us
    psum x1, waiting for transfers between devices, local(): lax.psum((row_stats[1] * rescale, rescale * (row_stats[2] + (row_stats[0]...  242 us
    pmax x1, blocking collectives, local(): top_all = lax.pmax(row_stats[0], ('kv', 'seq'))  101 us
    all_gather x1, waiting for transfers between devices, local(): shard_rows = lax.all_gather(packed, 'seq', axis=0, tiled=True)  73 us
    psum x1, waiting for transfers between devices, local(): lax.psum(jnp.dot(context, w_o, preferred_element_type=jnp.float32), 'kv')  69.3 us
  transfers between devices with their start and end apart: 4, of which 4 were waited for; matrix products, arithmetic and copies ran while one was open for 0% of the time, Pallas kernels for 0%

profile of v1, /device:TPU:1, one launch (start us, length us, event | category | flops | bytes accessed | tf_op | source)
XLA Modules:
  0.0 1167.0 jit_solution(17580678988797190828)
XLA Ops:
  7.3 0.9 copy.22
  9.1 1.4 fusion.16
  10.5 1.6 convolution_bitcast_fusion
  12.2 1.6 convolution_convert_fusion
  18.1 73.0 %all-gather.2.cloned.1.call-done = bf16[6144,128]{1,0:T(8,128)(2,1)} async-done(((bf16[192,128]{1,0:T(8,128)(2,1)}), bf16[6144,128]{1,0:T(8,128)(2,1)}) %all-gather.2.cloned.1.call-update) | async-done | bytes 1572880 | tf_op jit(solution)/shard_map/all_gather | solution.py:88
  91.2 21.6 %conditional.1 = (f32[1,4,192]{2,1,0:T(4,128)S(1)}, f32[1,4,192,64]{2,3,1,0:T(8,128)S(1)}) conditional(s32[]{:T(128)} %bitcast.9, (s32[6144]{0:T(1024)S(1)}, s32[6144]{0:T(1024)S(1)}, s32[192]{0:T(256)S(1)}, s32[192]{0:T(256)S(1)}, bf16[6144,128]{1,0:T(8,128)(2,1)}, /*index=5*/bf16[192,1,4,64]{0,3,2,1:T(8,128)(2,1)S(1)}) %tuple.16, () %tuple.17), branch_computations={%region_3.6_spmd, %region_6.7_spmd} | conditional | flops 1272839424 | bytes 66424336 | solution.py:118
  91.2 1.0 compare_and_fusion
  92.2 2.6 copy.25
  94.8 5.0 fusion
  99.8 6.3 fusion.7
  106.1 6.5 fusion.2
  112.8 1.6 fusion.37
  114.4 69.3 %all-reduce.4.cloned.1.call-done = f32[192,2048]{1,0:T(8,128)} async-done(((f32[192,2048]{1,0:T(8,128)}), f32[192,2048]{1,0:T(8,128)}) %all-reduce.4.cloned.1.call-update) | async-done | bytes 1572880 | tf_op jit(solution)/shard_map/psum | solution.py:129
  183.6 1.7 multiply_reduce_fusion.1
  185.4 1.7 multiply_convert_fusion
  187.1 8.6 stack.2
  195.7 9.8 all-to-all-start
  205.6 588.9 %all-to-all-done = bf16[32,192,2048]{2,1,0:T(8,128)(2,1)} async-done(((bf16[32,192,2048]{2,1,0:T(8,128)(2,1)}), bf16[32,192,2048]{2,1,0:T(8,128)(2,1)}, u32[]{:S(2)}, u32[]{:S(2)}) %all-to-all-start) | async-done | bytes 25165856 | tf_op jit(solution)/shard_map/all_to_all | solution.py:132
  794.5 14.5 %select_reduce_fusion.1 = (f32[6144]{0:T(1024)S(1)}, f32[6144,193]{0,1:T(8,128)}) fusion(pred[193]{0:T(512)(128)(4,1)S(1)} %broadcast_compare_fusion, bf16[6144,2048]{1,0:T(8,128)(2,1)} %bitcast.19, bf16[2048,193]{0,1:T(8,128)(2,1)S(1)} %copy-done.6), kind=kOutput, calls=%fused_computation.24 | convolution fusion | flops 4860555264 | bytes 30724288 | tf_op jit(solution)/shard_map/dot_general | solution.py:134
  809.0 101.5 %pmax.7 = f32[6144]{0:T(1024)S(1)} all-reduce(f32[6144]{0:T(1024)S(1)} %get-tuple-element.53), channel_id=1, replica_groups=mesh['kv'=8,'seq'=32] {'kv','seq'}, use_global_device_ids=true, to_apply=%region_12.13 | all-reduce | flops 6144 | bytes 49152 | tf_op jit(solution)/shard_map/pmax | solution.py:141
  910.5 4.9 multiply_reduce_fusion
  916.0 242.3 %all-reduce.6.cloned.1.call-done = (f32[6144]{0:T(1024)}, f32[6144]{0:T(1024)}, f32[6144]{0:T(1024)}) async-done(((f32[6144]{0:T(1024)}, f32[6144]{0:T(1024)}, f32[6144]{0:T(1024)}), (f32[6144]{0:T(1024)}, f32[6144]{0:T(1024)}, f32[6144]{0:T(1024)})) %all-reduce.6.cloned.1.call-update) | async-done | bytes 73744 | tf_op jit(solution)/shard_map/psum | solution.py:143
  1158.3 0.7 log.4
  1159.1 1.4 fusion.32
  (48 shorter events, 4.7 us)
Async XLA Ops:
  7.2 105.6 %copy-start = (bf16[256,2048]{1,0:T(8,128)(2,1)S(1)}, bf16[256,2048]{1,0:T(8,128)(2,1)}, u32[]{:S(2)}) copy-start(bf16[256,2048]{1,0:T(8,128)(2,1)} %param.18) | copy-start | bytes 3145732
  7.2 10.2 copy-start.2
  7.2 10.2 copy-start.7
  7.2 10.2 copy-start.5
  7.2 84.0 %all-gather.2.cloned.1.call-start = ((), (), s32[]{:S(2)}) async-start(), calls=%async_computation.1 | async-start | bytes 1622016 | tf_op jit(solution)/shard_map/all_gather | solution.py:88
  14.8 168.9 %all-reduce.4.cloned.1.call-start = ((), (), s32[]{:S(2)}) async-start(), calls=%async_computation.2 | async-start | bytes 3145728 | tf_op jit(solution)/shard_map/psum | solution.py:129
  112.7 72.6 %copy-start.4 = (f32[2048]{0:T(1024)S(1)}, f32[2048]{0:T(1024)}, u32[]{:S(2)}) copy-start(f32[2048]{0:T(1024)} %param.19) | copy-start | bytes 24580
  195.7 9.9 copy-start.8
  195.7 598.8 %copy-start.6 = (bf16[2048,193]{0,1:T(8,128)(2,1)S(1)}, bf16[2048,193]{0,1:T(8,128)(2,1)}, u32[]{:S(2)}) copy-start(bf16[2048,193]{0,1:T(8,128)(2,1)} %param.20) | copy-start | bytes 2371588
  195.7 598.8 %all-to-all-start = ((bf16[32,192,2048]{2,1,0:T(8,128)(2,1)}), bf16[32,192,2048]{2,1,0:T(8,128)(2,1)}, u32[]{:S(2)}, u32[]{:S(2)}) async-start(bf16[32,192,2048]{2,1,0:T(8,128)(2,1)} %stack.2), calls=%async_computation | async-start | bytes 50331648 | tf_op jit(solution)/shard_map/all_to_all | solution.py:132
  205.5 952.8 %all-reduce.6.cloned.1.call-start = ((), (), s32[]{:S(2)}) async-start(), calls=%async_computation.3 | async-start | bytes 147456 | tf_op jit(solution)/shard_map/psum | solution.py:143
  794.5 116.0 %copy-start.3 = (s32[6144]{0:T(1024)S(1)}, s32[6144]{0:T(1024)}, u32[]{:S(2)}) copy-start(s32[6144]{0:T(1024)} %param.22) | copy-start | bytes 73732
  794.5 365.9 %copy-start.1 = (bf16[256,2048]{1,0:T(8,128)(2,1)S(1)}, bf16[256,2048]{1,0:T(8,128)(2,1)}, u32[]{:S(2)}) copy-start(bf16[256,2048]{1,0:T(8,128)(2,1)} %param.18) | copy-start | bytes 3145732
Sparse Core Ops, SparseCore 0:
  14.9 76.2 all-gather.1
  114.5 69.0 all-reduce.3
  916.1 242.1 all-reduce.5
